TPU v7x, 512 devices: a whole 4x8x8 slice. The times are simulated.
512 devices in a mesh: seq: 64 (over y, x, core), fsdp: 8 (over z).
Axes of the slice: x: 4, y: 8, z: 8, core: 2. Of those that a mesh axis runs over, the one named last changes fastest.
Arguments:
- queries: bfloat16 [32768, 2048], P('seq', 'fsdp'), may hold values from -6 to 6
- keys: bfloat16 [32768, 2048], P('seq', 'fsdp'), may hold values from -6 to 6
- values: bfloat16 [32768, 2048], P('seq', 'fsdp'), may hold values from -6 to 6
- feature_weight: bfloat16 [16, 128, 128], P(None, 'fsdp', 'seq'), may hold values from -0.5 to 0.5
- norm_gain: bfloat16 [16, 128], P('fsdp'), may hold values from 0.099609375 to 1.8984375
- doc_bounds: int32 [4, 2], replicated, may hold values from 0 to 256, as said below
- out_grad: bfloat16 [32768, 2048], P('seq', 'fsdp'), may hold values from -6 to 6
Outputs:
- mixed: bfloat16 [32768, 2048], P('seq', 'fsdp')
- query_grad: bfloat16 [32768, 2048], P('seq', 'fsdp')
- key_grad: bfloat16 [32768, 2048], P('seq', 'fsdp')
- value_grad: bfloat16 [32768, 2048], P('seq', 'fsdp')
- weight_grad: float32 [16, 128, 128], P(None, 'fsdp', 'seq')
- gain_grad: float32 [16, 128], P('fsdp')
Inputs may be any that keep to these rules, and one draw needn't show every extreme that they name: `doc_bounds`: the rows list the 4 documents in order: column 0 is the first block and column 1 the block after the last; the first document starts at block 0, each ends where the next starts, the last ends at block 256; every document holds one block or more of 128 tokens.
All inputs are finite; a program needn't handle non-finite values.
Results may differ from a plain program's by a relative error of at most 0.015.
Values may be sent and summed in bfloat16 or wider, within the bound.
No kernel may reach another device: no remote copies, remote signals or barrier semaphores. Data moves between devices by JAX's collectives and lax.ppermute only.
A program may use at most 64 MiB of HBM per device.

v0:
```python
import jax
import jax.numpy as jnp
from jax import lax
from jax.sharding import PartitionSpec as P

HS = 128
BLK = 128
epsilon = 1.0


def carried_in(shard, axis, join, neutral, backward):
    count = lax.axis_size(axis)
    place = lax.axis_index(axis)
    ahead = count - 1 - place if backward else place
    gathered = jax.tree.map(
        lambda a, kind: lax.all_gather(a.astype(kind), axis), shard, (jnp.bfloat16, jnp.bfloat16)
    )
    state = jax.tree.map(lambda a, e: jnp.zeros_like(a) + jnp.asarray(e, a.dtype), shard, neutral)

    def one(hop, state):
        source = count - 1 - hop if backward else hop
        return join(
            state,
            jax.tree.map(
                lambda a, own: lax.dynamic_index_in_dim(a, source, 0, False).astype(own.dtype),
                gathered,
                shard,
            ),
        )

    return lax.fori_loop(0, ahead, one, state)


def chain_states(earlier, later):
    early_state, early_flag = earlier
    late_state, late_flag = later
    return (
        jnp.where(late_flag > 0.0, late_state, early_state + late_state),
        jnp.maximum(early_flag, late_flag),
    )


def project(rows, weight):
    return jnp.einsum("bthd,hde->bthe", rows, weight, preferred_element_type=jnp.float32).astype(
        jnp.bfloat16
    )


def local(queries, keys, values, feature_weight, norm_gain, doc_bounds, out_grad):
    rows_full = lax.all_gather(feature_weight, "seq", axis=2, tiled=True)
    weight_local = lax.all_to_all(rows_full, "fsdp", split_axis=0, concat_axis=1, tiled=True)
    head_count = weight_local.shape[0]
    tokens_here = queries.shape[0]
    block_count = tokens_here // BLK
    block_shape = (block_count, BLK, head_count, HS)
    query_blocks = queries.reshape(block_shape)
    key_blocks = keys.reshape(block_shape)
    value_blocks = values.reshape(block_shape)
    qfeat = project(query_blocks, weight_local)
    kfeat = project(key_blocks, weight_local)
    first_block = lax.axis_index("seq") * block_count
    block_ids = first_block + jnp.arange(block_count, dtype=jnp.int32)
    starts = doc_bounds[:, 0]
    starts_here = jnp.any(starts[None, :] == block_ids[:, None], axis=1)
    opened = jnp.cumsum(starts_here.astype(jnp.int32))
    reach_left = opened == 0
    reach_right = opened[-1] - opened == 0
    has_start = jnp.any(starts_here).astype(jnp.float32)
    updates = jnp.einsum("bthe,bthf->bhef", kfeat, value_blocks, preferred_element_type=jnp.float32)
    zero_state = jnp.zeros(updates.shape[1:], jnp.float32)
    zero_flag = jnp.zeros((), jnp.float32)
    running = zero_state
    prefix_list = []
    for position in range(block_count):
        held = jnp.where(starts_here[position], zero_state, running)
        prefix_list.append(held)
        running = held + updates[position]
    entering, _ = carried_in(
        (running, has_start), "seq", chain_states, (zero_state, zero_flag), False
    )
    states = jnp.stack(prefix_list) + jnp.where(
        reach_left[:, None, None, None], entering[None], 0.0
    )
    state_half = states.astype(jnp.bfloat16)
    causal = jnp.arange(BLK)[:, None] >= jnp.arange(BLK)[None, :]
    scores = jnp.einsum("bthe,bshe->bhts", qfeat, kfeat, preferred_element_type=jnp.float32)
    prob_half = jnp.where(causal, scores, 0.0).astype(jnp.bfloat16)
    mixed_f = jnp.einsum("bthe,bhef->bthf", qfeat, state_half, preferred_element_type=jnp.float32)
    mixed_f = mixed_f + jnp.einsum(
        "bhts,bshf->bthf", prob_half, value_blocks, preferred_element_type=jnp.float32
    )
    gains = norm_gain.astype(jnp.float32)
    inverse = lax.rsqrt(jnp.mean(mixed_f * mixed_f, axis=-1, keepdims=True) + epsilon)
    mixed = (mixed_f * inverse * gains).astype(jnp.bfloat16)
    grad_y = out_grad.reshape(block_shape).astype(jnp.float32)
    scaled = grad_y * gains
    grad_mix = inverse * (
        scaled - mixed_f * inverse * inverse * jnp.mean(scaled * mixed_f, axis=-1, keepdims=True)
    )
    grad_half = grad_mix.astype(jnp.bfloat16)
    gain_part = jnp.sum(grad_y * mixed_f * inverse, axis=(0, 1))
    state_grads = jnp.einsum(
        "bthe,bthf->bhef", qfeat, grad_half, preferred_element_type=jnp.float32
    )
    running = zero_state
    suffix_list = [zero_state] * block_count
    for position in reversed(range(block_count)):
        suffix_list[position] = running
        running = jnp.where(starts_here[position], zero_state, running + state_grads[position])
    leaving, _ = carried_in(
        (running, has_start), "seq", chain_states, (zero_state, zero_flag), True
    )
    suffix = jnp.stack(suffix_list) + jnp.where(
        reach_right[:, None, None, None], leaving[None], 0.0
    )
    suffix_half = suffix.astype(jnp.bfloat16)
    dot_grads = jnp.einsum(
        "bthf,bshf->bhts", grad_half, value_blocks, preferred_element_type=jnp.float32
    )
    dot_half = jnp.where(causal, dot_grads, 0.0).astype(jnp.bfloat16)
    qfeat_grad = jnp.einsum(
        "bthf,bhef->bthe", grad_half, state_half, preferred_element_type=jnp.float32
    )
    qfeat_grad = (
        qfeat_grad
        + jnp.einsum("bhts,bshe->bthe", dot_half, kfeat, preferred_element_type=jnp.float32)
    ).astype(jnp.bfloat16)
    kfeat_grad = jnp.einsum(
        "bshf,bhef->bshe", value_blocks, suffix_half, preferred_element_type=jnp.float32
    )
    kfeat_grad = (
        kfeat_grad
        + jnp.einsum("bhts,bthe->bshe", dot_half, qfeat, preferred_element_type=jnp.float32)
    ).astype(jnp.bfloat16)
    value_grad = jnp.einsum(
        "bshe,bhef->bshf", kfeat, suffix_half, preferred_element_type=jnp.float32
    )
    value_grad = (
        value_grad
        + jnp.einsum("bhts,bthf->bshf", prob_half, grad_half, preferred_element_type=jnp.float32)
    ).astype(jnp.bfloat16)
    query_grad = jnp.einsum(
        "bthe,hde->bthd", qfeat_grad, weight_local, preferred_element_type=jnp.float32
    ).astype(jnp.bfloat16)
    key_grad = jnp.einsum(
        "bthe,hde->bthd", kfeat_grad, weight_local, preferred_element_type=jnp.float32
    ).astype(jnp.bfloat16)
    weight_part = jnp.einsum(
        "bthd,bthe->hde", query_blocks, qfeat_grad, preferred_element_type=jnp.float32
    )
    weight_part = weight_part + jnp.einsum(
        "bthd,bthe->hde", key_blocks, kfeat_grad, preferred_element_type=jnp.float32
    )
    weight_sum, gain_sum = lax.psum((weight_part, gain_part), "seq")
    column_width = weight_sum.shape[2] // lax.axis_size("seq")
    weight_columns = lax.dynamic_slice_in_dim(
        weight_sum, lax.axis_index("seq") * column_width, column_width, 2
    )
    owned_grad = lax.all_to_all(weight_columns, "fsdp", split_axis=1, concat_axis=0, tiled=True)
    factor = (lax.axis_size("seq") * tokens_here) ** (-0.5)
    flat_shape = (tokens_here, head_count * HS)
    return (
        mixed.reshape(flat_shape),
        query_grad.reshape(flat_shape),
        key_grad.reshape(flat_shape),
        value_grad.reshape(flat_shape),
        owned_grad * factor,
        gain_sum * factor,
    )


def solution(mesh):
    placed = (
        P("seq", "fsdp"),
        P("seq", "fsdp"),
        P("seq", "fsdp"),
        P(None, "fsdp", "seq"),
        P("fsdp", None),
        P(),
        P("seq", "fsdp"),
    )
    return jax.shard_map(
        local,
        mesh=mesh,
        in_specs=placed,
        out_specs=(
            P("seq", "fsdp"),
            P("seq", "fsdp"),
            P("seq", "fsdp"),
            P("seq", "fsdp"),
            P(None, "fsdp", "seq"),
            P("fsdp", None),
        ),
        check_vma=False,
    )
```

profile of v0, /device:TPU:1, one launch (start us, length us, event | category | flops | bytes accessed | tf_op | source)
XLA Modules:
  0.0 827.8 jit_solution(3233053818263169173)
XLA Ops:
  8.0 53.9 %all_gather.19 = bf16[16,16,128]{1,0,2:T(8,128)(2,1)S(1)} all-gather(bf16[16,16,2]{1,0,2:T(8,128)(2,1)S(1)} %copy.146), channel_id=1, replica_groups=mesh['seq'=64,'fsdp'=8] {'seq'}, dimensions={2}, use_global_device_ids=true | all-gather | bytes 66560 | tf_op jit(solution)/shard_map/all_gather | solution.py:50
  61.8 1.1 copy.147
  62.9 8.9 %all-to-all-start = ((bf16[16,16,128]{2,1,0:T(8,128)(2,1)}), bf16[16,16,128]{2,1,0:T(8,128)(2,1)S(1)}, u32[]{:S(2)}, u32[]{:S(2)}) async-start(bf16[16,16,128]{2,1,0:T(8,128)(2,1)} %copy.147), calls=%async_computation | async-start | bytes 131072 | tf_op jit(solution)/shard_map/all_to_all | solution.py:51
  73.3 1.0 reshape.100
  74.3 1.0 reshape.101
  76.0 3.0 all-to-all-done
  79.5 2.5 fusion.43
  84.1 1.3 dynamic-slice
  86.1 125.5 %all-reduce = bf16[64]{0:T(256)(128)(2,1)S(1)} all-reduce(bf16[64]{0:T(256)(128)(2,1)S(1)} %dynamic-update-slice), channel_id=1, replica_groups=mesh['seq'=64,'fsdp'=8] {'seq'}, use_global_device_ids=true, to_apply=%add | all-reduce | flops 64 | bytes 256
  213.9 2.1 while.26
  215.1 0.9 add_select_fusion.4
  217.2 3.2 fusion.40
  220.8 1.2 fusion.48
  222.9 0.9 copy.160
  223.8 252.4 %psum.15 = f32[2,128]{1,0:T(2,128)S(1)} all-reduce(f32[2,128]{1,0:T(2,128)S(1)} %get-tuple-element.136), channel_id=1, replica_groups=mesh['seq'=64,'fsdp'=8] {'seq'}, use_global_device_ids=true, to_apply=%region_11.12 | all-reduce | flops 256 | bytes 2048 | tf_op jit(solution)/shard_map/psum | solution.py:154
  476.8 1.5 fusion.41
  478.3 1.9 copy_bitcast_fusion.2
  480.2 132.8 %while.27 = (s32[]{:T(128)}, f32[2,128,128]{2,1,0:T(8,128)S(1)}, s32[]{:T(128)}, bf16[64]{0:T(256)(128)(2,1)S(1)}, bf16[64,2,128,128]{3,2,1,0:T(8,128)(2,1)}, /*...) while((s32[]{:T(128)}, f32[2,128,128]{2,1,0:T(8,128)S(1)}, s32[]{:T(128)}, ...), condition=%wide.region_8.9_spmd, body=%wide.region_7.8_spmd.sunk | while | flops 98311 | bytes 327847 | solution.py:31
  481.4 0.9 add_select_fusion.5
  483.6 0.9 add_select_fusion.5
  485.7 0.9 add_select_fusion.5
  492.2 0.9 add_select_fusion.5
  494.3 0.9 add_select_fusion.5
  496.4 0.9 add_select_fusion.5
  498.6 0.9 add_select_fusion.5
  500.7 0.9 add_select_fusion.5
  502.9 0.9 add_select_fusion.5
  505.0 0.9 add_select_fusion.5
  532.8 0.9 add_select_fusion.5
  535.0 0.9 add_select_fusion.5
  537.1 0.9 add_select_fusion.5
  539.3 0.9 add_select_fusion.5
  541.4 0.9 add_select_fusion.5
  543.5 0.9 add_select_fusion.5
  545.7 0.9 add_select_fusion.5
  573.5 0.9 add_select_fusion.5
  575.7 0.9 add_select_fusion.5
  577.8 0.9 add_select_fusion.5
  580.0 0.9 add_select_fusion.5
  582.1 0.9 add_select_fusion.5
  584.2 0.9 add_select_fusion.5
  586.4 0.9 add_select_fusion.5
  613.0 1.4 fusion.29
  614.4 1.4 fusion.34
  616.2 0.9 fusion.14
  618.1 184.5 %all-reduce.3.cloned.1.call-done = f32[2,128,128]{1,2,0:T(8,128)} async-done(((f32[2,128,128]{1,2,0:T(8,128)}), f32[2,128,128]{1,2,0:T(8,128)}) %all-reduce.3.cloned.1.call-update) | async-done | bytes 131088 | tf_op jit(solution)/shard_map/psum | solution.py:154
  804.0 7.1 all-to-all-start.1
  812.0 8.5 %all-to-all-done.1 = f32[2,128,2]{2,0,1:T(2,128)S(1)} async-done(((f32[2,128,2]{2,0,1:T(2,128)}), f32[2,128,2]{2,0,1:T(2,128)S(1)}, u32[]{:S(2)}, u32[]{:S(2)}) %all-to-all-start.1) | async-done | bytes 2080 | tf_op jit(solution)/shard_map/all_to_all | solution.py:159
  (173 shorter events, 85.2 us)
Async XLA Ops:
  7.2 75.6 %copy-start.2 = (bf16[512,256]{1,0:T(8,128)(2,1)S(1)}, bf16[512,256]{1,0:T(8,128)(2,1)}, u32[]{:S(2)}) copy-start(bf16[512,256]{1,0:T(8,128)(2,1)} %param.11) | copy-start | bytes 786436
  7.2 76.4 %copy-start.1 = (bf16[512,256]{1,0:T(8,128)(2,1)S(1)}, bf16[512,256]{1,0:T(8,128)(2,1)}, u32[]{:S(2)}) copy-start(bf16[512,256]{1,0:T(8,128)(2,1)} %param.17) | copy-start | bytes 786436
  7.2 76.9 %copy-start.7 = (bf16[2,128]{1,0:T(2,128)(2,1)S(1)}, bf16[2,128]{1,0:T(2,128)(2,1)}, u32[]{:S(2)}) copy-start(bf16[2,128]{1,0:T(2,128)(2,1)} %param.15) | copy-start | bytes 1540
  62.9 16.1 %all-to-all-start = ((bf16[16,16,128]{2,1,0:T(8,128)(2,1)}), bf16[16,16,128]{2,1,0:T(8,128)(2,1)S(1)}, u32[]{:S(2)}, u32[]{:S(2)}) async-start(bf16[16,16,128]{2,1,0:T(8,128)(2,1)} %copy.147), calls=%async_computation | async-start | bytes 131072 | tf_op jit(solution)/shard_map/all_to_all | solution.py:51
  71.8 142.0 %all-gather.3.cloned.1.call-start = ((), (), s32[]{:S(2)}) async-start(), calls=%async_computation.2 | async-start | bytes 4259840 | tf_op jit(solution)/shard_map/all_gather | solution.py:16
  82.0 398.1 %all-gather.5.cloned.1.call-start = ((), (), s32[]{:S(2)}) async-start(), calls=%async_computation.3 | async-start | bytes 4259840 | tf_op jit(solution)/shard_map/all_gather | solution.py:16
  83.8 132.2 %copy-start.6 = (f32[1,2,128,128]{3,2,1,0:T(8,128)S(1)}, f32[1,2,128,128]{3,2,1,0:T(8,128)}, u32[]{:S(2)}) copy-start(f32[1,2,128,128]{3,2,1,0:T(8,128)} %get-tuple-element.165) | copy-start | bytes 393220
  212.9 3.7 copy-start.4
  216.0 6.3 copy-start.3
  220.4 582.1 %all-reduce.3.cloned.1.call-start = ((), (), s32[]{:S(2)}) async-start(), calls=%async_computation.4 | async-start | bytes 262144 | tf_op jit(solution)/shard_map/psum | solution.py:154
  223.8 390.6 %copy-start = (f32[1,2,128,128]{3,2,1,0:T(8,128)S(1)}, f32[1,2,128,128]{3,2,1,0:T(8,128)}, u32[]{:S(2)}) copy-start(f32[1,2,128,128]{3,2,1,0:T(8,128)} %get-tuple-element.161) | copy-start | bytes 393220
  478.3 134.7 %copy-start.5 = (f32[1,2,128,128]{3,2,1,0:T(8,128)}, f32[1,2,128,128]{3,2,1,0:T(8,128)S(1)}, u32[]{:S(2)}) copy-start(f32[1,2,128,128]{3,2,1,0:T(8,128)S(1)} %fusion.41) | copy-start | bytes 393220
  804.0 16.4 %all-to-all-start.1 = ((f32[2,128,2]{2,0,1:T(2,128)}), f32[2,128,2]{2,0,1:T(2,128)S(1)}, u32[]{:S(2)}, u32[]{:S(2)}) async-start(f32[2,128,2]{2,0,1:T(2,128)} %copy.179), calls=%async_computation.1 | async-start | bytes 262144 | tf_op jit(solution)/shard_map/all_to_all | solution.py:159
Sparse Core Ops, SparseCore 0:
  82.1 79.6 all-gather.2
  220.5 208.0 all-gather.4
  617.2 185.2 all-reduce.2
where the time goes:
time: 832 us; the launch traced here: 828 us
  blocking collectives  432 us (52%)
  waiting for transfers between devices  196 us (24%)
  other arithmetic  65.2 us (8%)
  local copies, waits for them, and re-layouts  52 us (6%)
  loops' own time  43.2 us (5%)
  starting transfers between devices  16.1 us (2%)
  between operations  14.8 us (2%)
  matrix products  8.74 us (1%)
    psum x1, blocking collectives, local(): weight_sum, gain_sum = lax.psum((weight_part, gain_part), 'seq')  252 us
    psum x1, waiting for transfers between devices, local(): weight_sum, gain_sum = lax.psum((weight_part, gain_part), 'seq')  184 us
    unnamed x1, blocking collectives  126 us
    select_n x63, other arithmetic, chain_states(): jnp.where(late_flag > 0.0, late_state, early_state + late_state)  54.7 us
    all_gather x1, blocking collectives, local(): rows_full = lax.all_gather(feature_weight, 'seq', axis=2, tiled=True)  53.9 us
    another operation x2, loops' own time, carried_in(): return lax.fori_loop(0, ahead, one, state)  43.2 us
    dynamic_slice x63, local copies, waits for them, and re-layouts, one(): lax.dynamic_index_in_dim(a, source, 0, False).astype(own.dtype)  37 us
  transfers between devices with their start and end apart: 5, of which 3 were waited for; matrix products, arithmetic and copies ran while one was open for 2% of the time, Pallas kernels for 0%

commit v1 on v0

--- a/solution.py
+++ b/solution.py
@@ -47,7 +47,10 @@
 
 
 def local(queries, keys, values, feature_weight, norm_gain, doc_bounds, out_grad):
-    rows_full = lax.all_gather(feature_weight, "seq", axis=2, tiled=True)
+    count_2 = lax.axis_size("seq")
+    blocks = jnp.stack([feature_weight for _ in range(count_2)])
+    blocks = lax.all_to_all(blocks, "seq", split_axis=0, concat_axis=0)
+    rows_full = jnp.concatenate(blocks, axis=2)
     weight_local = lax.all_to_all(rows_full, "fsdp", split_axis=0, concat_axis=1, tiled=True)
     head_count = weight_local.shape[0]
     tokens_here = queries.shape[0]

time: 832 us -> 801 us (0.963)
  blocking collectives: 432 us -> 377 us
  starting transfers between devices: 16.1 us -> 28.9 us
  waiting for transfers between devices: 196 us -> 205 us
    all_gather x1 -> x0, blocking collectives: 53.9 us -> none  [local(): rows_full = lax.all_gather(feature_weight, 'seq', axis=2, tiled=True)]
    all_to_all x0 -> x1, starting transfers between devices: none -> 11.6 us  [local(): blocks = lax.all_to_all(blocks, 'seq', split_axis=0, concat_axis=0)]
    all_to_all x0 -> x1, waiting for transfers between devices: none -> 9.4 us  [local(): blocks = lax.all_to_all(blocks, 'seq', split_axis=0, concat_axis=0)]
  transfers between devices with their start and end apart: 5 -> 6, of which waited for: 3 -> 4; matrix products, arithmetic and copies ran while one was open for 2% -> 2% of each run, Pallas kernels for 0% -> 0%
where the time goes in v1:
time: 801 us; the launch traced here: 796 us
  blocking collectives  377 us (47%)
  waiting for transfers between devices  205 us (26%)
  other arithmetic  65.4 us (8%)
  local copies, waits for them, and re-layouts  53.5 us (7%)
  loops' own time  43.1 us (5%)
  starting transfers between devices  28.9 us (4%)
  between operations  14.8 us (2%)
  matrix products  8.74 us (1%)
    psum x1, blocking collectives, local(): weight_sum, gain_sum = lax.psum((weight_part, gain_part), 'seq')  252 us
    psum x1, waiting for transfers between devices, local(): weight_sum, gain_sum = lax.psum((weight_part, gain_part), 'seq')  183 us
    unnamed x1, blocking collectives  126 us
    select_n x63, other arithmetic, chain_states(): jnp.where(late_flag > 0.0, late_state, early_state + late_state)  54.7 us
    another operation x2, loops' own time, carried_in(): return lax.fori_loop(0, ahead, one, state)  43.1 us
    dynamic_slice x63, local copies, waits for them, and re-layouts, one(): lax.dynamic_index_in_dim(a, source, 0, False).astype(own.dtype)  37 us
  transfers between devices with their start and end apart: 6, of which 4 were waited for; matrix products, arithmetic and copies ran while one was open for 2% of the time, Pallas kernels for 0%

profile of v1, /device:TPU:1, one launch (start us, length us, event | category | flops | bytes accessed | tf_op | source)
XLA Modules:
  0.0 796.4 jit_solution(11939907995261651431)
XLA Ops:
  8.0 1.1 reshape.131
  9.1 11.6 %all-to-all-start = ((bf16[64,2,256]{2,1,0:T(2,128)(2,1)}), bf16[64,2,256]{2,1,0:T(2,128)(2,1)S(1)}, u32[]{:S(2)}, u32[]{:S(2)}) async-start(bf16[64,2,256]{2,1,0:T(2,128)(2,1)} %reshape.131), calls=%async_computation | async-start | bytes 131072 | tf_op jit(solution)/shard_map/all_to_all | solution.py:52
  21.4 9.4 %all-to-all-done = bf16[64,2,256]{2,1,0:T(2,128)(2,1)S(1)} async-done(((bf16[64,2,256]{2,1,0:T(2,128)(2,1)}), bf16[64,2,256]{2,1,0:T(2,128)(2,1)S(1)}, u32[]{:S(2)}, u32[]{:S(2)}) %all-to-all-start) | async-done | bytes 65568 | tf_op jit(solution)/shard_map/all_to_all | solution.py:52
  31.2 1.1 copy.116
  32.3 10.0 %all-to-all-start.1 = ((bf16[16,16,128]{2,1,0:T(8,128)(2,1)}), bf16[16,16,128]{2,1,0:T(8,128)(2,1)S(1)}, u32[]{:S(2)}, u32[]{:S(2)}) async-start(bf16[16,16,128]{2,1,0:T(8,128)(2,1)} %copy.116), calls=%async_computation.1 | async-start | bytes 131072 | tf_op jit(solution)/shard_map/all_to_all | solution.py:54
  43.0 1.0 reshape.110
  44.1 1.0 reshape.111
  45.7 3.8 all-to-all-done.1
  50.0 2.6 fusion.43
  54.7 1.3 dynamic-slice
  56.7 125.7 %all-reduce = bf16[64]{0:T(256)(128)(2,1)S(1)} all-reduce(bf16[64]{0:T(256)(128)(2,1)S(1)} %dynamic-update-slice), channel_id=1, replica_groups=mesh['seq'=64,'fsdp'=8] {'seq'}, use_global_device_ids=true, to_apply=%add | all-reduce | flops 64 | bytes 256
  184.6 2.1 while.26
  187.9 3.3 fusion.40
  191.6 1.2 fusion.48
  193.7 0.9 copy.129
  194.6 251.6 %psum.15 = f32[2,128]{1,0:T(2,128)S(1)} all-reduce(f32[2,128]{1,0:T(2,128)S(1)} %get-tuple-element.136), channel_id=1, replica_groups=mesh['seq'=64,'fsdp'=8] {'seq'}, use_global_device_ids=true, to_apply=%region_11.12 | all-reduce | flops 256 | bytes 2048 | tf_op jit(solution)/shard_map/psum | solution.py:157
  446.8 1.5 fusion.41
  448.4 1.9 copy_bitcast_fusion.2
  450.2 132.8 %while.27 = (s32[]{:T(128)}, f32[2,128,128]{2,1,0:T(8,128)S(1)}, s32[]{:T(128)}, bf16[64]{0:T(256)(128)(2,1)S(1)}, bf16[64,2,128,128]{3,2,1,0:T(8,128)(2,1)}, /*...) while((s32[]{:T(128)}, f32[2,128,128]{2,1,0:T(8,128)S(1)}, s32[]{:T(128)}, ...), condition=%wide.region_8.9_spmd, body=%wide.region_7.8_spmd.sunk | while | flops 98311 | bytes 327847 | solution.py:31
  451.5 0.9 add_select_fusion.5
  453.7 0.9 add_select_fusion.5
  455.8 0.9 add_select_fusion.5
  457.9 0.9 add_select_fusion.5
  460.1 0.9 add_select_fusion.5
  462.2 0.9 add_select_fusion.5
  464.4 0.9 add_select_fusion.5
  492.2 0.9 add_select_fusion.5
  494.3 0.9 add_select_fusion.5
  496.5 0.9 add_select_fusion.5
  498.6 0.9 add_select_fusion.5
  500.8 0.9 add_select_fusion.5
  502.9 0.9 add_select_fusion.5
  505.1 0.9 add_select_fusion.5
  532.9 0.9 add_select_fusion.5
  535.0 0.9 add_select_fusion.5
  537.2 0.9 add_select_fusion.5
  539.3 0.9 add_select_fusion.5
  541.5 0.9 add_select_fusion.5
  543.6 0.9 add_select_fusion.5
  545.7 0.9 add_select_fusion.5
  573.6 0.9 add_select_fusion.5
  575.7 0.9 add_select_fusion.5
  583.0 1.4 fusion.29
  584.4 1.4 fusion.34
  586.3 0.9 fusion.14
  588.1 182.9 %all-reduce.3.cloned.1.call-done = f32[2,128,128]{1,2,0:T(8,128)} async-done(((f32[2,128,128]{1,2,0:T(8,128)}), f32[2,128,128]{1,2,0:T(8,128)}) %all-reduce.3.cloned.1.call-update) | async-done | bytes 131088 | tf_op jit(solution)/shard_map/psum | solution.py:157
  772.6 7.1 all-to-all-start.2
  780.5 8.5 %all-to-all-done.2 = f32[2,128,2]{2,0,1:T(2,128)S(1)} async-done(((f32[2,128,2]{2,0,1:T(2,128)}), f32[2,128,2]{2,0,1:T(2,128)S(1)}, u32[]{:S(2)}, u32[]{:S(2)}) %all-to-all-start.2) | async-done | bytes 2080 | tf_op jit(solution)/shard_map/all_to_all | solution.py:162
  (177 shorter events, 87.3 us)
Async XLA Ops:
  7.2 46.2 %copy-start.2 = (bf16[512,256]{1,0:T(8,128)(2,1)S(1)}, bf16[512,256]{1,0:T(8,128)(2,1)}, u32[]{:S(2)}) copy-start(bf16[512,256]{1,0:T(8,128)(2,1)} %param.11) | copy-start | bytes 786436
  7.2 47.0 %copy-start.1 = (bf16[512,256]{1,0:T(8,128)(2,1)S(1)}, bf16[512,256]{1,0:T(8,128)(2,1)}, u32[]{:S(2)}) copy-start(bf16[512,256]{1,0:T(8,128)(2,1)} %param.17) | copy-start | bytes 786436
  8.0 46.7 %copy-start.7 = (bf16[2,128]{1,0:T(2,128)(2,1)S(1)}, bf16[2,128]{1,0:T(2,128)(2,1)}, u32[]{:S(2)}) copy-start(bf16[2,128]{1,0:T(2,128)(2,1)} %param.15) | copy-start | bytes 1540
  9.1 21.7 %all-to-all-start = ((bf16[64,2,256]{2,1,0:T(2,128)(2,1)}), bf16[64,2,256]{2,1,0:T(2,128)(2,1)S(1)}, u32[]{:S(2)}, u32[]{:S(2)}) async-start(bf16[64,2,256]{2,1,0:T(2,128)(2,1)} %reshape.131), calls=%async_computation | async-start | bytes 131072 | tf_op jit(solution)/shard_map/all_to_all | solution.py:52
  32.3 17.3 %all-to-all-start.1 = ((bf16[16,16,128]{2,1,0:T(8,128)(2,1)}), bf16[16,16,128]{2,1,0:T(8,128)(2,1)S(1)}, u32[]{:S(2)}, u32[]{:S(2)}) async-start(bf16[16,16,128]{2,1,0:T(8,128)(2,1)} %copy.116), calls=%async_computation.1 | async-start | bytes 131072 | tf_op jit(solution)/shard_map/all_to_all | solution.py:54
  42.3 142.3 %all-gather.3.cloned.1.call-start = ((), (), s32[]{:S(2)}) async-start(), calls=%async_computation.3 | async-start | bytes 4259840 | tf_op jit(solution)/shard_map/all_gather | solution.py:16
  52.6 397.6 %all-gather.5.cloned.1.call-start = ((), (), s32[]{:S(2)}) async-start(), calls=%async_computation.4 | async-start | bytes 4259840 | tf_op jit(solution)/shard_map/all_gather | solution.py:16
  54.5 132.3 %copy-start.6 = (f32[1,2,128,128]{3,2,1,0:T(8,128)S(1)}, f32[1,2,128,128]{3,2,1,0:T(8,128)}, u32[]{:S(2)}) copy-start(f32[1,2,128,128]{3,2,1,0:T(8,128)} %get-tuple-element.165) | copy-start | bytes 393220
  183.7 3.7 copy-start.4
  186.8 6.4 copy-start.3
  191.2 579.8 %all-reduce.3.cloned.1.call-start = ((), (), s32[]{:S(2)}) async-start(), calls=%async_computation.5 | async-start | bytes 262144 | tf_op jit(solution)/shard_map/psum | solution.py:157
  194.6 389.8 %copy-start = (f32[1,2,128,128]{3,2,1,0:T(8,128)S(1)}, f32[1,2,128,128]{3,2,1,0:T(8,128)}, u32[]{:S(2)}) copy-start(f32[1,2,128,128]{3,2,1,0:T(8,128)} %get-tuple-element.161) | copy-start | bytes 393220
  448.4 134.7 %copy-start.5 = (f32[1,2,128,128]{3,2,1,0:T(8,128)}, f32[1,2,128,128]{3,2,1,0:T(8,128)S(1)}, u32[]{:S(2)}) copy-start(f32[1,2,128,128]{3,2,1,0:T(8,128)S(1)} %fusion.41) | copy-start | bytes 393220
  772.6 16.4 %all-to-all-start.2 = ((f32[2,128,2]{2,0,1:T(2,128)}), f32[2,128,2]{2,0,1:T(2,128)S(1)}, u32[]{:S(2)}, u32[]{:S(2)}) async-start(f32[2,128,2]{2,0,1:T(2,128)} %copy.148), calls=%async_computation.2 | async-start | bytes 262144 | tf_op jit(solution)/shard_map/all_to_all | solution.py:162
Sparse Core Ops, SparseCore 0:
  52.8 75.5 all-gather.2
  191.3 205.3 all-gather.4
  587.3 183.7 all-reduce.2
